TPU v7x, 128 devices: a whole 4x4x4 slice. The times are simulated.
128 devices in a mesh: col: 8 (over y, z_hi), pair: 16 (over x, z_lo, core).
Axes of the slice: x: 4, y: 4, z: 4 (z_hi: 2, z_lo: 2; z = z_hi * 2 + z_lo), core: 2. Of those that a mesh axis runs over, the one named last changes fastest.
Arguments:
- integrals: bfloat16 [512, 128, 128], P('pair', 'col'), may hold values from -6 to 6
- pno_energy: float32 [512, 128], P('pair'), may hold values from 0.5 to 4
- shift: float32 [512], P('pair'), may hold values from 0.5 to 2
- intersections: bfloat16 [512, 128, 128, 128], P('pair', 'col'), may hold values from -0.09375 to 0.09375
- links: int32 [512, 128], P('pair', 'col'), may hold values from 0 to 63
- counts: int32 [512], P('pair'), may hold values from 1 to 128, as said below
- column_of: int32 [512], P('pair'), may hold values from 0 to 63
Outputs:
- amplitudes: float32 [512, 128, 128], P('pair', 'col')
- pair_energy: float32 [512], P('pair')
Inputs may be any that keep to these rules, and one draw needn't show every extreme that they name: Pair p couples through its first counts[p] slots; later slots are unused.
All inputs are finite; a program needn't handle non-finite values.
Results may differ from a plain program's by a relative error of at most 0.0012.
Values may be sent and summed in bfloat16 or wider, within the bound.
No kernel may reach another device: no remote copies, remote signals or barrier semaphores. Data moves between devices by JAX's collectives and lax.ppermute only.
A program may use at most 192 MiB of HBM per device.

v0:
```python
import jax
import jax.numpy as jnp
from jax import lax
from jax.sharding import PartitionSpec as P

COL_DEV = 8
SWEEPS = 3


def per_device(integrals, pno_energy, shift, intersections, links, counts, column_of):
    pair_dev = integrals.shape[0]
    row_count = integrals.shape[1]
    width = integrals.shape[2]
    slot_dev = intersections.shape[1]
    col_size = lax.axis_size("col")
    ncol_all = COL_DEV * col_size
    rank = lax.axis_index("col")
    row_energy = lax.dynamic_slice_in_dim(pno_energy, rank * row_count, row_count, 1)
    denom = row_energy[:, :, None] + pno_energy[:, None, :] + shift[:, None, None]
    kfloat = integrals.astype(jnp.float32)
    amplitudes = -kfloat / denom
    one_hot = (jnp.arange(ncol_all, dtype=jnp.int32)[:, None] == column_of[None, :]).astype(
        jnp.float32
    )
    own_tiles, own_links = (intersections, links)
    slot_ids = rank * slot_dev + jnp.arange(slot_dev, dtype=jnp.int32)
    own_live = (slot_ids[None, :] < counts[:, None]).astype(jnp.float32)
    for sweep in range(SWEEPS):
        contrib = jnp.dot(
            one_hot,
            amplitudes.reshape(pair_dev, row_count * width),
            precision=lax.Precision.HIGHEST,
        )
        contrib = contrib.reshape(ncol_all, row_count, width)
        totals = lax.psum(contrib, "pair")
        colamp = lax.all_gather(totals.astype(jnp.bfloat16), "col", axis=1, tiled=True)
        selected = colamp[own_links]
        left = jnp.einsum(
            "pmab,pmbc->pmac", own_tiles, selected, preferred_element_type=jnp.float32
        ).astype(jnp.bfloat16)
        right = jnp.einsum("pmac,pmdc->pmad", left, own_tiles, preferred_element_type=jnp.float32)
        partial_sum = jnp.sum(right * own_live[:, :, None, None], axis=1)
        coupled = lax.psum_scatter(partial_sum, "col", scatter_dimension=1, tiled=True)
        amplitudes = -(kfloat + coupled) / denom
    pair_energy = lax.psum(jnp.sum(kfloat * amplitudes, axis=(1, 2)), "col")
    return (amplitudes, pair_energy)


def solution(mesh):
    placed = (
        P("pair", "col", None),
        P("pair", None),
        P("pair"),
        P("pair", "col", None, None),
        P("pair", "col"),
        P("pair"),
        P("pair"),
    )
    return jax.shard_map(
        per_device,
        mesh=mesh,
        in_specs=placed,
        out_specs=(P("pair", "col", None), P("pair")),
        check_vma=False,
    )
```

profile of v0, /device:TPU:0, one launch (start us, length us, event | category | flops | bytes accessed | tf_op | source)
XLA Modules:
  0.0 745.7 jit_solution(13268401989379443307)
XLA Ops:
  7.2 0.0 all-gather.4.cloned.1.call-start
  7.2 0.8 constant_dynamic-slice_fusion
  8.0 1.1 fusion.18
  9.1 1.1 fusion.32
  10.3 62.5 %all-reduce.3 = bf16[64,16,128]{2,0,1:T(8,128)(2,1)} all-reduce(f32[64,16,128]{2,0,1:T(8,128)S(1)} %fusion.32), channel_id=1, replica_groups=mesh['col'=8,'pair'=16] {'pair'}, use_global_device_ids=true, to_apply=%region_0.0 | all-reduce | flops 131072 | bytes 786432 | tf_op jit(solution)/shard_map/psum | solution.py:35
  72.7 0.0 all-gather.4.cloned.1.call-update
  72.8 0.0 reduce-scatter.4.cloned.1.call-start
  72.8 0.7 compare_select_fusion
  73.5 0.1 copy.17
  73.6 0.1 reshape.61
  73.7 0.7 compare_convert_fusion
  74.4 52.9 %all-gather.4.cloned.1.call-done = bf16[64,128,128]{2,0,1:T(8,128)(2,1)} async-done(((bf16[64,16,128]{2,0,1:T(8,128)(2,1)}), bf16[64,128,128]{2,0,1:T(8,128)(2,1)}) %all-gather.4.cloned.1.call-update) | async-done | bytes 2097168 | tf_op jit(solution)/shard_map/all_gather | solution.py:36
  127.3 2.9 copy.18
  130.2 13.9 %gather_fusion = bf16[512,128,128]{2,1,0:T(8,128)(2,1)} fusion(bf16[64,128,128]{2,1,0:T(8,128)(2,1)S(1)} %copy.18, s32[1024]{0:T(1024)S(1)} %pad_clamp_fusion), kind=kCustom, calls=%fused_computation | custom fusion | bytes 33556480 | tf_op jit(solution)/shard_map/gather | solution.py:37
  144.1 0.0 copy-start
  144.1 29.2 %multiply_reduce_fusion.2 = f32[32,128,128]{2,1,0:T(8,128)} fusion(f32[32,16]{1,0:T(8,128)S(1)} %compare_convert_fusion, bf16[32,16,128,128]{3,2,1,0:T(8,128)(2,1)} %param.10, bf16[32,16,128,128]{3,2,1,0:T(8,128)(2,1)} %bitcast.57), kind=kOutput, calls=%fused_computation.5 | convolution fusion | flops 4319608832 | bytes 35653632 | tf_op jit(solution)/shard_map/pmac,pmdc->pmad/dot_general | solution.py:41
  173.4 0.0 reduce-scatter.4.cloned.1.call-update
  173.4 0.0 all-gather.6.cloned.1.call-start
  173.4 74.5 %reduce-scatter.4.cloned.1.call-done = f32[32,16,128]{2,1,0:T(8,128)} async-done(((f32[32,128,128]{2,1,0:T(8,128)}), f32[32,16,128]{2,1,0:T(8,128)}) %reduce-scatter.4.cloned.1.call-update) | async-done | bytes 262160 | tf_op jit(solution)/shard_map/reduce_scatter | solution.py:43
  247.9 0.0 copy-done
  247.9 0.0 copy-done.1
  247.9 0.0 copy-done.2
  247.9 1.1 fusion.20
  249.1 0.0 copy-done.3
  249.1 0.5 fusion.29
  249.6 59.6 %all-reduce.4 = bf16[64,16,128]{2,0,1:T(8,128)(2,1)} all-reduce(f32[64,16,128]{2,0,1:T(8,128)S(1)} %fusion.29), channel_id=1, replica_groups=mesh['col'=8,'pair'=16] {'pair'}, use_global_device_ids=true, to_apply=%region_3.0 | all-reduce | flops 131072 | bytes 786432 | tf_op jit(solution)/shard_map/psum | solution.py:35
  309.1 0.0 all-gather.6.cloned.1.call-update
  309.2 0.2 reduce-scatter.6.cloned.1.call-start
  309.4 51.7 %all-gather.6.cloned.1.call-done = bf16[64,128,128]{2,0,1:T(8,128)(2,1)} async-done(((bf16[64,16,128]{2,0,1:T(8,128)(2,1)}), bf16[64,128,128]{2,0,1:T(8,128)(2,1)}) %all-gather.6.cloned.1.call-update) | async-done | bytes 2097168 | tf_op jit(solution)/shard_map/all_gather | solution.py:36
  361.1 2.9 copy.22
  364.0 13.9 %gather_fusion.1 = bf16[512,128,128]{2,1,0:T(8,128)(2,1)} fusion(bf16[64,128,128]{2,1,0:T(8,128)(2,1)S(1)} %copy.22, s32[1024]{0:T(1024)S(1)} %pad_clamp_fusion), kind=kCustom, calls=%fused_computation.1 | custom fusion | bytes 33556480 | tf_op jit(solution)/shard_map/gather | solution.py:37
  377.9 29.2 %multiply_reduce_fusion.1 = f32[32,128,128]{2,1,0:T(8,128)} fusion(f32[32,16]{1,0:T(8,128)S(1)} %compare_convert_fusion, bf16[32,16,128,128]{3,2,1,0:T(8,128)(2,1)} %param.10, bf16[32,16,128,128]{3,2,1,0:T(8,128)(2,1)} %bitcast.58), kind=kOutput, calls=%fused_computation.4 | convolution fusion | flops 4319608832 | bytes 35653632 | tf_op jit(solution)/shard_map/pmac,pmdc->pmad/dot_general | solution.py:41
  407.1 0.0 reduce-scatter.6.cloned.1.call-update
  407.1 0.0 all-gather.8.cloned.1.call-start
  407.2 74.3 %reduce-scatter.6.cloned.1.call-done = f32[32,16,128]{2,1,0:T(8,128)} async-done(((f32[32,128,128]{2,1,0:T(8,128)}), f32[32,16,128]{2,1,0:T(8,128)}) %reduce-scatter.6.cloned.1.call-update) | async-done | bytes 262160 | tf_op jit(solution)/shard_map/reduce_scatter | solution.py:43
  481.5 1.1 fusion.22
  482.7 0.5 fusion.26
  483.2 59.7 %all-reduce.5 = bf16[64,16,128]{2,0,1:T(8,128)(2,1)} all-reduce(f32[64,16,128]{2,0,1:T(8,128)S(1)} %fusion.26), channel_id=1, replica_groups=mesh['col'=8,'pair'=16] {'pair'}, use_global_device_ids=true, to_apply=%region_6.0 | all-reduce | flops 131072 | bytes 786432 | tf_op jit(solution)/shard_map/psum | solution.py:35
  542.8 0.0 all-gather.8.cloned.1.call-update
  542.8 0.3 reduce-scatter.8.cloned.1.call-start
  543.1 51.6 %all-gather.8.cloned.1.call-done = bf16[64,128,128]{2,0,1:T(8,128)(2,1)} async-done(((bf16[64,16,128]{2,0,1:T(8,128)(2,1)}), bf16[64,128,128]{2,0,1:T(8,128)(2,1)}) %all-gather.8.cloned.1.call-update) | async-done | bytes 2097168 | tf_op jit(solution)/shard_map/all_gather | solution.py:36
  594.8 2.9 copy.26
  597.7 13.9 %gather_fusion.2 = bf16[512,128,128]{2,1,0:T(8,128)(2,1)} fusion(bf16[64,128,128]{2,1,0:T(8,128)(2,1)S(1)} %copy.26, s32[1024]{0:T(1024)S(1)} %pad_clamp_fusion), kind=kCustom, calls=%fused_computation.2 | custom fusion | bytes 33556480 | tf_op jit(solution)/shard_map/gather | solution.py:37
  611.6 29.2 %multiply_reduce_fusion = f32[32,128,128]{2,1,0:T(8,128)} fusion(f32[32,16]{1,0:T(8,128)S(1)} %compare_convert_fusion, bf16[32,16,128,128]{3,2,1,0:T(8,128)(2,1)} %param.10, bf16[32,16,128,128]{3,2,1,0:T(8,128)(2,1)} %bitcast.56), kind=kOutput, calls=%fused_computation.3 | convolution fusion | flops 4319608832 | bytes 35653632 | tf_op jit(solution)/shard_map/pmac,pmdc->pmad/dot_general | solution.py:41
  640.8 0.0 reduce-scatter.8.cloned.1.call-update
  640.8 74.3 %reduce-scatter.8.cloned.1.call-done = f32[32,16,128]{2,1,0:T(8,128)} async-done(((f32[32,128,128]{2,1,0:T(8,128)}), f32[32,16,128]{2,1,0:T(8,128)}) %reduce-scatter.8.cloned.1.call-update) | async-done | bytes 262160 | tf_op jit(solution)/shard_map/reduce_scatter | solution.py:43
  715.2 2.2 fusion.25
  717.3 21.5 %psum.31 = f32[32]{0:T(128)} all-reduce(f32[32]{0:T(128)S(1)} %get-tuple-element.2), channel_id=1, replica_groups=mesh['col'=8,'pair'=16] {'col'}, use_global_device_ids=true, to_apply=%region_10.0 | all-reduce | flops 32 | bytes 256 | tf_op jit(solution)/shard_map/psum | solution.py:45
  (5 shorter events, 0.0 us)
Async XLA Ops:
  7.2 120.1 %all-gather.4.cloned.1.call-start = ((), (), s32[]{:S(2)}) async-start(), calls=%async_computation.3 | async-start | bytes 2359296 | tf_op jit(solution)/shard_map/all_gather | solution.py:36
  72.8 175.2 %reduce-scatter.4.cloned.1.call-start = ((), (), s32[]{:S(2)}) async-start(), calls=%async_computation.4 | async-start | bytes 2359296 | tf_op jit(solution)/shard_map/reduce_scatter | solution.py:43
  144.1 103.8 %copy-start = (bf16[32,16,128]{2,1,0:T(8,128)(2,1)S(1)}, bf16[32,16,128]{2,1,0:T(8,128)(2,1)}, u32[]{:S(2)}) copy-start(bf16[32,16,128]{2,1,0:T(8,128)(2,1)} %param.7) | copy-start | bytes 393220
  144.1 103.8 %copy-start.1 = (f32[32,128]{1,0:T(8,128)S(1)}, f32[32,128]{1,0:T(8,128)}, u32[]{:S(2)}) copy-start(f32[32,128]{1,0:T(8,128)} %param.8) | copy-start | bytes 49156
  144.1 103.8 %copy-start.2 = (f32[32]{0:T(128)S(1)}, f32[32]{0:T(128)}, u32[]{:S(2)}) copy-start(f32[32]{0:T(128)} %param.9) | copy-start | bytes 388
  144.1 104.9 %copy-start.3 = (s32[32]{0:T(128)S(1)}, s32[32]{0:T(128)}, u32[]{:S(2)}) copy-start(s32[32]{0:T(128)} %param.13) | copy-start | bytes 388
  173.4 187.7 %all-gather.6.cloned.1.call-start = ((), (), s32[]{:S(2)}) async-start(), calls=%async_computation.5 | async-start | bytes 2359296 | tf_op jit(solution)/shard_map/all_gather | solution.py:36
  309.2 172.4 %reduce-scatter.6.cloned.1.call-start = ((), (), s32[]{:S(2)}) async-start(), calls=%async_computation.6 | async-start | bytes 2359296 | tf_op jit(solution)/shard_map/reduce_scatter | solution.py:43
  407.1 187.6 %all-gather.8.cloned.1.call-start = ((), (), s32[]{:S(2)}) async-start(), calls=%async_computation.7 | async-start | bytes 2359296 | tf_op jit(solution)/shard_map/all_gather | solution.py:36
  542.8 172.3 %reduce-scatter.8.cloned.1.call-start = ((), (), s32[]{:S(2)}) async-start(), calls=%async_computation.8 | async-start | bytes 2359296 | tf_op jit(solution)/shard_map/reduce_scatter | solution.py:43
Sparse Core Ops, SparseCore 0:
  72.9 54.3 all-gather.3
  173.5 74.3 reduce-scatter.3
  309.3 51.7 all-gather.5
  407.3 74.2 reduce-scatter.5
  543.0 51.7 all-gather.7
  640.9 74.1 reduce-scatter.7
where the time goes:
time: 746 us
  waiting for transfers between devices  379 us (51%)
  blocking collectives  203 us (27%)
  matrix products  89.7 us (12%)
  local copies, waits for them, and re-layouts  51.5 us (7%)
  between operations  14.2 us (2%)
    reduce_scatter x3, waiting for transfers between devices, per_device(): lax.psum_scatter(partial_sum, 'col', scatter_dimension=1, tiled=True)  223 us
    psum x3, blocking collectives, per_device(): totals = lax.psum(contrib, 'pair')  182 us
    all_gather x3, waiting for transfers between devices, per_device(): lax.all_gather(totals.astype(jnp.bfloat16), 'col', axis=1, tiled=True)  156 us
    dot_general x3, matrix products, per_device(): jnp.einsum('pmac,pmdc->pmad', left, own_tiles, preferred_element_type=jnp...  87.6 us
    gather x3, local copies, waits for them, and re-layouts, per_device(): selected = colamp[own_links]  41.7 us
    psum x1, blocking collectives, per_device(): pair_energy = lax.psum(jnp.sum(kfloat * amplitudes, axis=(1, 2)), 'col')  21.5 us
  transfers between devices with their start and end apart: 6, of which 6 were waited for; matrix products, arithmetic and copies ran while one was open for 0% of the time, Pallas kernels for 0%

commit v1 on v0

--- a/solution.py
+++ b/solution.py
@@ -32,7 +32,7 @@
             precision=lax.Precision.HIGHEST,
         )
         contrib = contrib.reshape(ncol_all, row_count, width)
-        totals = lax.psum(contrib, "pair")
+        totals = jnp.sum(lax.all_gather(contrib, "pair"), axis=0)
         colamp = lax.all_gather(totals.astype(jnp.bfloat16), "col", axis=1, tiled=True)
         selected = colamp[own_links]
         left = jnp.einsum(

time: 746 us -> 752 us (level)
  blocking collectives: 203 us -> 21.5 us
  waiting for transfers between devices: 379 us -> 553 us
  other arithmetic: 6.93 us -> 20.1 us
    psum x3 -> x0, blocking collectives: 182 us -> none  [per_device(): totals = lax.psum(contrib, 'pair')]
    all_gather x0 -> x3, waiting for transfers between devices: none -> 156 us  [per_device(): totals = jnp.sum(lax.all_gather(contrib, 'pair'), axis=0)]
    all_gather x3, waiting for transfers between devices: 156 us -> 174 us  [per_device(): lax.all_gather(totals.astype(jnp.bfloat16), 'col', axis=1, tiled=True)]
    reduce_sum x0 -> x3, other arithmetic: none -> 13.2 us  [per_device(): totals = jnp.sum(lax.all_gather(contrib, 'pair'), axis=0)]
    all_gather x3 -> x0, local copies, waits for them, and re-layouts: 8.83 us -> none  [per_device(): lax.all_gather(totals.astype(jnp.bfloat16), 'col', axis=1, tiled=True)]
  transfers between devices with their start and end apart: 6 -> 9, of which waited for: 6 -> 9; matrix products, arithmetic and copies ran while one was open for 0% -> 0% of each run, Pallas kernels for 0% -> 0%
where the time goes in v1:
time: 752 us
  waiting for transfers between devices  553 us (74%)
  matrix products  92.3 us (12%)
  local copies, waits for them, and re-layouts  50 us (7%)
  blocking collectives  21.5 us (3%)
  other arithmetic  20.1 us (3%)
  between operations  13.9 us (2%)
    reduce_scatter x3, waiting for transfers between devices, per_device(): lax.psum_scatter(partial_sum, 'col', scatter_dimension=1, tiled=True)  223 us
    all_gather x3, waiting for transfers between devices, per_device(): lax.all_gather(totals.astype(jnp.bfloat16), 'col', axis=1, tiled=True)  174 us
    all_gather x3, waiting for transfers between devices, per_device(): totals = jnp.sum(lax.all_gather(contrib, 'pair'), axis=0)  156 us
    dot_general x3, matrix products, per_device(): jnp.einsum('pmac,pmdc->pmad', left, own_tiles, preferred_element_type=jnp...  87.6 us
    gather x3, local copies, waits for them, and re-layouts, per_device(): selected = colamp[own_links]  46.4 us
    psum x1, blocking collectives, per_device(): pair_energy = lax.psum(jnp.sum(kfloat * amplitudes, axis=(1, 2)), 'col')  21.5 us
  transfers between devices with their start and end apart: 9, of which 9 were waited for; matrix products, arithmetic and copies ran while one was open for 0% of the time, Pallas kernels for 0%

profile of v1, /device:TPU:0, one launch (start us, length us, event | category | flops | bytes accessed | tf_op | source)
XLA Modules:
  0.0 751.8 jit_solution(5269219326829976941)
XLA Ops:
  7.2 0.0 all-gather.16.cloned.1.call-start
  7.2 0.8 constant_dynamic-slice_fusion
  8.0 1.1 fusion.18
  9.1 2.0 fusion.32
  11.1 0.0 all-gather.16.cloned.1.call-update
  11.1 0.0 all-gather.10.cloned.1.call-start
  11.2 54.7 %all-gather.16.cloned.1.call-done = f32[1024,16,128]{2,0,1:T(8,128)} async-done(((f32[64,16,128]{2,0,1:T(8,128)}), f32[1024,16,128]{2,0,1:T(8,128)}) %all-gather.16.cloned.1.call-update) | async-done | bytes 8388624 | tf_op jit(solution)/shard_map/all_gather | solution.py:35
  65.9 4.4 reduce_sum.63
  70.3 0.9 copy.68
  71.2 0.0 all-gather.10.cloned.1.call-update
  71.2 0.0 reduce-scatter.4.cloned.1.call-start
  71.3 0.7 compare_select_fusion
  72.0 0.1 copy.25
  72.0 0.1 reshape.155
  72.1 0.7 compare_convert_fusion
  72.9 56.9 %all-gather.10.cloned.1.call-done = bf16[64,128,128]{2,1,0:T(8,128)(2,1)} async-done(((bf16[64,16,128]{2,1,0:T(8,128)(2,1)}), bf16[64,128,128]{2,1,0:T(8,128)(2,1)}) %all-gather.10.cloned.1.call-update) | async-done | bytes 2097168 | tf_op jit(solution)/shard_map/all_gather | solution.py:36
  129.8 15.5 %gather_fusion = bf16[512,128,128]{2,1,0:T(8,128)(2,1)} fusion(bf16[64,128,128]{2,1,0:T(8,128)(2,1)} %all-gather.10.cloned.1.call-done, s32[1024]{0:T(1024)S(1)} %pad_clamp_fusion), kind=kCustom, calls=%fused_computation | custom fusion | bytes 33556480 | tf_op jit(solution)/shard_map/gather | solution.py:37
  145.3 29.2 %multiply_reduce_fusion.2 = f32[32,128,128]{2,1,0:T(8,128)} fusion(f32[32,16]{1,0:T(8,128)S(1)} %compare_convert_fusion, bf16[32,16,128,128]{3,2,1,0:T(8,128)(2,1)} %param.10, bf16[32,16,128,128]{3,2,1,0:T(8,128)(2,1)} %bitcast.62), kind=kOutput, calls=%fused_computation.5 | convolution fusion | flops 4319608832 | bytes 35653632 | tf_op jit(solution)/shard_map/pmac,pmdc->pmad/dot_general | solution.py:41
  174.5 0.0 reduce-scatter.4.cloned.1.call-update
  174.5 0.0 all-gather.18.cloned.1.call-start
  174.6 74.4 %reduce-scatter.4.cloned.1.call-done = f32[32,16,128]{2,1,0:T(8,128)} async-done(((f32[32,128,128]{2,1,0:T(8,128)}), f32[32,16,128]{2,1,0:T(8,128)}) %reduce-scatter.4.cloned.1.call-update) | async-done | bytes 262160 | tf_op jit(solution)/shard_map/reduce_scatter | solution.py:43
  249.0 1.1 fusion.20
  250.2 1.3 fusion.29
  251.5 0.0 all-gather.18.cloned.1.call-update
  251.5 0.0 all-gather.12.cloned.1.call-start
  251.6 50.7 %all-gather.18.cloned.1.call-done = f32[1024,16,128]{2,0,1:T(8,128)} async-done(((f32[64,16,128]{2,0,1:T(8,128)}), f32[1024,16,128]{2,0,1:T(8,128)}) %all-gather.18.cloned.1.call-update) | async-done | bytes 8388624 | tf_op jit(solution)/shard_map/all_gather | solution.py:35
  302.3 4.4 reduce_sum.65
  306.7 0.9 copy.67
  307.5 0.0 all-gather.12.cloned.1.call-update
  307.6 0.2 reduce-scatter.6.cloned.1.call-start
  307.8 58.4 %all-gather.12.cloned.1.call-done = bf16[64,128,128]{2,1,0:T(8,128)(2,1)} async-done(((bf16[64,16,128]{2,1,0:T(8,128)(2,1)}), bf16[64,128,128]{2,1,0:T(8,128)(2,1)}) %all-gather.12.cloned.1.call-update) | async-done | bytes 2097168 | tf_op jit(solution)/shard_map/all_gather | solution.py:36
  366.2 15.5 %gather_fusion.1 = bf16[512,128,128]{2,1,0:T(8,128)(2,1)} fusion(bf16[64,128,128]{2,1,0:T(8,128)(2,1)} %all-gather.12.cloned.1.call-done, s32[1024]{0:T(1024)S(1)} %pad_clamp_fusion), kind=kCustom, calls=%fused_computation.1 | custom fusion | bytes 33556480 | tf_op jit(solution)/shard_map/gather | solution.py:37
  381.6 29.2 %multiply_reduce_fusion.1 = f32[32,128,128]{2,1,0:T(8,128)} fusion(f32[32,16]{1,0:T(8,128)S(1)} %compare_convert_fusion, bf16[32,16,128,128]{3,2,1,0:T(8,128)(2,1)} %param.10, bf16[32,16,128,128]{3,2,1,0:T(8,128)(2,1)} %bitcast.63), kind=kOutput, calls=%fused_computation.4 | convolution fusion | flops 4319608832 | bytes 35653632 | tf_op jit(solution)/shard_map/pmac,pmdc->pmad/dot_general | solution.py:41
  410.9 0.0 all-gather.20.cloned.1.call-start
  410.9 74.3 %reduce-scatter.6.cloned.1.call-done = f32[32,16,128]{2,1,0:T(8,128)} async-done(((f32[32,128,128]{2,1,0:T(8,128)}), f32[32,16,128]{2,1,0:T(8,128)}) %reduce-scatter.6.cloned.1.call-update) | async-done | bytes 262160 | tf_op jit(solution)/shard_map/reduce_scatter | solution.py:43
  485.3 1.1 fusion.22
  486.4 1.3 fusion.26
  487.8 0.0 all-gather.14.cloned.1.call-start
  487.8 50.7 %all-gather.20.cloned.1.call-done = f32[1024,16,128]{2,0,1:T(8,128)} async-done(((f32[64,16,128]{2,0,1:T(8,128)}), f32[1024,16,128]{2,0,1:T(8,128)}) %all-gather.20.cloned.1.call-update) | async-done | bytes 8388624 | tf_op jit(solution)/shard_map/all_gather | solution.py:35
  538.5 4.4 reduce_sum.67
  542.9 0.9 copy.66
  543.8 0.3 reduce-scatter.8.cloned.1.call-start
  544.1 58.3 %all-gather.14.cloned.1.call-done = bf16[64,128,128]{2,1,0:T(8,128)(2,1)} async-done(((bf16[64,16,128]{2,1,0:T(8,128)(2,1)}), bf16[64,128,128]{2,1,0:T(8,128)(2,1)}) %all-gather.14.cloned.1.call-update) | async-done | bytes 2097168 | tf_op jit(solution)/shard_map/all_gather | solution.py:36
  602.4 15.5 %gather_fusion.2 = bf16[512,128,128]{2,1,0:T(8,128)(2,1)} fusion(bf16[64,128,128]{2,1,0:T(8,128)(2,1)} %all-gather.14.cloned.1.call-done, s32[1024]{0:T(1024)S(1)} %pad_clamp_fusion), kind=kCustom, calls=%fused_computation.2 | custom fusion | bytes 33556480 | tf_op jit(solution)/shard_map/gather | solution.py:37
  617.9 29.2 %multiply_reduce_fusion = f32[32,128,128]{2,1,0:T(8,128)} fusion(f32[32,16]{1,0:T(8,128)S(1)} %compare_convert_fusion, bf16[32,16,128,128]{3,2,1,0:T(8,128)(2,1)} %param.10, bf16[32,16,128,128]{3,2,1,0:T(8,128)(2,1)} %bitcast.61), kind=kOutput, calls=%fused_computation.3 | convolution fusion | flops 4319608832 | bytes 35653632 | tf_op jit(solution)/shard_map/pmac,pmdc->pmad/dot_general | solution.py:41
  647.1 74.5 %reduce-scatter.8.cloned.1.call-done = f32[32,16,128]{2,1,0:T(8,128)} async-done(((f32[32,128,128]{2,1,0:T(8,128)}), f32[32,16,128]{2,1,0:T(8,128)}) %reduce-scatter.8.cloned.1.call-update) | async-done | bytes 262160 | tf_op jit(solution)/shard_map/reduce_scatter | solution.py:43
  721.6 2.2 fusion.25
  723.8 21.5 %psum.7 = f32[32]{0:T(128)} all-reduce(f32[32]{0:T(128)S(1)} %get-tuple-element.2), channel_id=1, replica_groups=mesh['col'=8,'pair'=16] {'col'}, use_global_device_ids=true, to_apply=%region_10.0 | all-reduce | flops 32 | bytes 256 | tf_op jit(solution)/shard_map/psum | solution.py:45
  (14 shorter events, 0.1 us)
Async XLA Ops:
  7.2 58.7 %all-gather.16.cloned.1.call-start = ((), (), s32[]{:S(2)}) async-start(), calls=%async_computation.9 | async-start | bytes 8912896 | tf_op jit(solution)/shard_map/all_gather | solution.py:35
  11.1 118.7 %all-gather.10.cloned.1.call-start = ((), (), s32[]{:S(2)}) async-start(), calls=%async_computation.3 | async-start | bytes 2359296 | tf_op jit(solution)/shard_map/all_gather | solution.py:36
  71.2 177.8 %reduce-scatter.4.cloned.1.call-start = ((), (), s32[]{:S(2)}) async-start(), calls=%async_computation.4 | async-start | bytes 2359296 | tf_op jit(solution)/shard_map/reduce_scatter | solution.py:43
  145.3 103.7 %copy-start = (bf16[32,16,128]{2,1,0:T(8,128)(2,1)S(1)}, bf16[32,16,128]{2,1,0:T(8,128)(2,1)}, u32[]{:S(2)}) copy-start(bf16[32,16,128]{2,1,0:T(8,128)(2,1)} %param.7) | copy-start | bytes 393220
  145.3 103.7 %copy-start.1 = (f32[32,128]{1,0:T(8,128)S(1)}, f32[32,128]{1,0:T(8,128)}, u32[]{:S(2)}) copy-start(f32[32,128]{1,0:T(8,128)} %param.8) | copy-start | bytes 49156
  145.3 103.7 %copy-start.2 = (f32[32]{0:T(128)S(1)}, f32[32]{0:T(128)}, u32[]{:S(2)}) copy-start(f32[32]{0:T(128)} %param.9) | copy-start | bytes 388
  145.3 104.9 %copy-start.3 = (s32[32]{0:T(128)S(1)}, s32[32]{0:T(128)}, u32[]{:S(2)}) copy-start(s32[32]{0:T(128)} %param.13) | copy-start | bytes 388
  174.5 127.7 %all-gather.18.cloned.1.call-start = ((), (), s32[]{:S(2)}) async-start(), calls=%async_computation.10 | async-start | bytes 8912896 | tf_op jit(solution)/shard_map/all_gather | solution.py:35
  251.5 114.6 %all-gather.12.cloned.1.call-start = ((), (), s32[]{:S(2)}) async-start(), calls=%async_computation.5 | async-start | bytes 2359296 | tf_op jit(solution)/shard_map/all_gather | solution.py:36
  307.6 177.7 %reduce-scatter.6.cloned.1.call-start = ((), (), s32[]{:S(2)}) async-start(), calls=%async_computation.6 | async-start | bytes 2359296 | tf_op jit(solution)/shard_map/reduce_scatter | solution.py:43
  410.9 127.6 %all-gather.20.cloned.1.call-start = ((), (), s32[]{:S(2)}) async-start(), calls=%async_computation.11 | async-start | bytes 8912896 | tf_op jit(solution)/shard_map/all_gather | solution.py:35
  487.8 114.6 %all-gather.14.cloned.1.call-start = ((), (), s32[]{:S(2)}) async-start(), calls=%async_computation.7 | async-start | bytes 2359296 | tf_op jit(solution)/shard_map/all_gather | solution.py:36
  543.8 177.8 %reduce-scatter.8.cloned.1.call-start = ((), (), s32[]{:S(2)}) async-start(), calls=%async_computation.8 | async-start | bytes 2359296 | tf_op jit(solution)/shard_map/reduce_scatter | solution.py:43
Sparse Core Ops, SparseCore 0:
  11.2 54.6 all-gather.15
  71.3 58.4 all-gather.9
  174.7 74.3 reduce-scatter.3
  251.6 50.5 all-gather.17
  307.7 58.4 all-gather.11
  411.0 74.2 reduce-scatter.5
  487.9 50.5 all-gather.19
  543.9 58.4 all-gather.13
  647.2 74.3 reduce-scatter.7
